TPU v7x, 32 devices: a whole 2x2x4 slice. The times are simulated.
32 devices in a mesh: grp: 2 (over x), date: 16 (over z, y, core).
Axes of the slice: x: 2, y: 2, z: 4, core: 2. Of those that a mesh axis runs over, the one named last changes fastest.
Arguments:
- slc: bfloat16 [16, 2, 128, 2048], P('date', None, 'grp'), parts along dimension 2, may hold values from -6 to 6
- pairs: int32 [64, 2], replicated, may hold values from 0 to 15, as said below
- inverse: bfloat16 [15, 64], replicated, may hold values from -6 to 6
Outputs:
- series: float32 [15, 32, 128], P(None, ('grp', 'date')), parts along dimension 1
There are 2 independent parts, one for each index of `grp`. A program takes and returns all parts, laid end to end along the dimension named above; an argument that names none is the same for every part. Nothing has to cross between parts.
Inputs may be any that keep to these rules, and one draw needn't show every extreme that they name: pairs[p,0] < pairs[p,1] for every pair.
All inputs are finite; a program needn't handle non-finite values.
Results may differ from a plain program's by a relative error of at most 0.0003.
Values may be sent and summed in bfloat16 or wider, within the bound.
No kernel may reach another device: no remote copies, remote signals or barrier semaphores. Data moves between devices by JAX's collectives and lax.ppermute only.
A program may use at most 128 MiB of HBM per device.

v0:
```python
import jax
import jax.numpy as jnp
from jax import lax
from jax.sharding import PartitionSpec as P

LOOK_R = 4
LOOK_C = 16


def coherence(first, second):
    first = first.astype(jnp.float32)
    second = second.astype(jnp.float32)
    cross = first[:, 1] * second[:, 0] - first[:, 0] * second[:, 1]
    power_ref = first[:, 0] * first[:, 0] + first[:, 1] * first[:, 1]
    power_sec = second[:, 0] * second[:, 0] + second[:, 1] * second[:, 1]
    stacked = jnp.stack([cross, power_ref, power_sec])
    three, count, rows, cols = stacked.shape
    rowsum = stacked.reshape(three, count, rows // LOOK_R, LOOK_R, cols).sum(axis=3)
    window = (jnp.arange(cols)[:, None] // LOOK_C == jnp.arange(cols // LOOK_C)[None, :]).astype(
        jnp.float32
    )
    looked = jnp.dot(rowsum, window, precision=lax.Precision.HIGHEST)
    return looked[0] / jnp.sqrt(looked[1] * looked[2] + 1e-06)


def invert(inverse, proxy):
    return jnp.einsum(
        "sp,pxy->sxy", inverse.astype(jnp.float32), proxy, precision=lax.Precision.HIGHEST
    )


def per_device(slc, pairs, inverse):
    stripes = lax.all_to_all(slc, "date", split_axis=2, concat_axis=0, tiled=True)
    first = jnp.take(stripes, pairs[:, 0], axis=0)
    second = jnp.take(stripes, pairs[:, 1], axis=0)
    proxy = coherence(first, second)
    return invert(inverse, proxy)


def solution(mesh):
    in_specs = (P("date", None, "grp", None), P(), P())
    out_specs = P(None, ("grp", "date"), None)
    return jax.shard_map(
        per_device, mesh=mesh, in_specs=in_specs, out_specs=out_specs, check_vma=False
    )
```

profile of v0, /device:TPU:0, one launch (start us, length us, event | category | flops | bytes accessed | tf_op | source)
XLA Modules:
  0.0 41.9 jit_solution(5127418015980830979)
XLA Ops:
  0.0 0.0 copy-start
  0.0 0.0 copy-start.1
  0.0 2.4 %copy.26 = bf16[1,2,64,2048]{3,1,0,2:T(2,128)(2,1)} copy(bf16[1,2,64,2048]{3,2,1,0:T(8,128)(2,1)} %param.5) | data formatting | bytes 1048576 | tf_op args[0]
  2.4 7.4 %all-to-all-start = ((bf16[1,2,64,2048]{3,1,0,2:T(2,128)(2,1)}), bf16[1,2,64,2048]{3,1,0,2:T(2,128)(2,1)S(1)}, u32[]{:S(2)}, u32[]{:S(2)}) async-start(bf16[1,2,64,2048]{3,1,0,2:T(2,128)(2,1)} %copy.26), calls=%async_computation | async-start | bytes 1048576 | tf_op jit(solution)/shard_map/all_to_all | solution.py:33
  9.8 0.0 copy-done.1
  9.9 14.2 %all-to-all-done = bf16[1,2,64,2048]{3,1,0,2:T(2,128)(2,1)S(1)} async-done(((bf16[1,2,64,2048]{3,1,0,2:T(2,128)(2,1)}), bf16[1,2,64,2048]{3,1,0,2:T(2,128)(2,1)S(1)}, u32[]{:S(2)}, u32[]{:S(2)}) %all-to-all-start) | async-done | bytes 524320 | tf_op jit(solution)/shard_map/all_to_all | solution.py:33
  24.1 0.3 copy.38
  24.4 2.4 %gather_fusion = bf16[64,2,4,2048]{3,2,1,0:T(4,128)(2,1)S(1)} fusion(bf16[16,2,4,2048]{3,2,1,0:T(4,128)(2,1)S(1)} %bitcast.30, s32[1024]{0:T(1024)S(1)} %pad_clamp_fusion.1), kind=kCustom, calls=%fused_computation.clone | custom fusion | bytes 4194560 | tf_op jit(solution)/shard_map/jit(_take)/gather | solution.py:34
  26.7 3.6 %gather_fusion.1 = bf16[64,2,4,2048]{3,2,1,0:T(4,128)(2,1)} fusion(bf16[16,2,4,2048]{3,2,1,0:T(4,128)(2,1)S(1)} %bitcast.31, s32[1024]{0:T(1024)S(1)} %pad_clamp_fusion), kind=kCustom, calls=%fused_computation.1.clone | custom fusion | bytes 4194560 | tf_op jit(solution)/shard_map/jit(_take)/gather | solution.py:35
  30.3 7.5 %fusion = (f32[64,2,4,2048]{3,0,2,1:T(8,128)S(1)}, f32[64,2,4,2048]{3,0,2,1:T(8,128)S(1)}) fusion(bf16[64,2,4,2048]{3,2,1,0:T(4,128)(2,1)} %gather_fusion.1, pred[64]{0:T(512)(128)(4,1)S(1)} %get-tuple-element.13, bf16[64,2,4,2048]{3,2,1,0:T(4,128)(2,1)S(1)} %gather_fusion, pred[64]{0:T(512)(128)(4,1)S(1)} %get-tuple-element.6), kind=kLoop, calls=%fused_computation.4 | loop fusion | flops 4194304 | bytes 12583040 | tf_op jit(solution)/shard_map/convert_element_type | solution.py:12
  37.8 1.6 %subtract_bitcast_fusion = (f32[1,64,4,2048]{3,1,2,0:T(8,128)S(1)}, f32[1,64,4,2048]{3,1,2,0:T(8,128)S(1)}, f32[1,64,4,2048]{3,1,2,0:T(8,128)S(1)}) fusion(f32[64,2,4,2048]{3,0,2,1:T(8,128)S(1)} %get-tuple-element.15, f32[64,2,4,2048]{3,0,2,1:T(8,128)S(1)} %get-tuple-element.16), kind=kLoop, calls=%fused_computation.9 | loop fusion | flops 4718592 | bytes 14680064 | tf_op jit(solution)/shard_map/sub | solution.py:13
  39.5 0.7 %maximum_reduce_fusion = f32[3,64,2048]{2,1,0:T(8,128)S(1)} fusion(f32[1,64,4,2048]{3,1,2,0:T(8,128)S(1)} %get-tuple-element.12, f32[1,64,4,2048]{3,1,2,0:T(8,128)S(1)} %get-tuple-element.11, f32[1,64,4,2048]{3,1,2,0:T(8,128)S(1)} %get-tuple-element.10), kind=kLoop, calls=%fused_computation.2 | loop fusion | flops 4325376 | bytes 7864320 | tf_op jit(solution)/shard_map/reduce_sum | solution.py:18
  40.1 1.0 %fusion.3 = f32[3,64,128]{2,1,0:T(8,128)S(1)} fusion(f32[3,64,2048]{2,1,0:T(8,128)S(1)} %maximum_reduce_fusion, s32[2048]{0:T(1024)S(1)} %add_select_fusion), kind=kOutput, calls=%fused_computation.13 | convolution fusion | flops 604241920 | bytes 1679360 | tf_op jit(solution)/shard_map/dot_general | solution.py:22
  41.2 0.0 copy-done
  41.2 0.1 convolution_bitcast_fusion
  41.3 0.6 %copy.30 = f32[15,1,128]{2,1,0:T(1,128)} copy(f32[15,1,128]{2,0,1:T(8,128)S(1)} %convolution_bitcast_fusion) | data formatting | bytes 15360 | tf_op jit(solution)/shard_map/sp,pxy->sxy/dot_general | solution.py:27
  (4 shorter events, 0.0 us)
Async XLA Ops:
  0.0 41.2 %copy-start = (bf16[15,64]{1,0:T(8,128)(2,1)S(1)}, bf16[15,64]{1,0:T(8,128)(2,1)}, u32[]{:S(2)}) copy-start(bf16[15,64]{1,0:T(8,128)(2,1)} %param.7) | copy-start | bytes 5764
  0.0 9.8 %copy-start.1 = (s32[64,2]{0,1:T(2,128)S(1)}, s32[64,2]{0,1:T(2,128)}, u32[]{:S(2)}) copy-start(s32[64,2]{0,1:T(2,128)} %param.6) | copy-start | bytes 1540
  2.4 21.7 %all-to-all-start = ((bf16[1,2,64,2048]{3,1,0,2:T(2,128)(2,1)}), bf16[1,2,64,2048]{3,1,0,2:T(2,128)(2,1)S(1)}, u32[]{:S(2)}, u32[]{:S(2)}) async-start(bf16[1,2,64,2048]{3,1,0,2:T(2,128)(2,1)} %copy.26), calls=%async_computation | async-start | bytes 1048576 | tf_op jit(solution)/shard_map/all_to_all | solution.py:33
where the time goes:
time: 42.2 us; the launch traced here: 41.9 us
  waiting for transfers between devices  14.2 us (34%)
  other arithmetic  9.83 us (23%)
  local copies, waits for them, and re-layouts  9.23 us (22%)
  starting transfers between devices  7.41 us (18%)
  matrix products  1.16 us (3%)
    all_to_all x1, waiting for transfers between devices, per_device(): lax.all_to_all(slc, 'date', split_axis=2, concat_axis=0, tiled=True)  14.2 us
    convert_element_type x1, other arithmetic, coherence(): second = second.astype(jnp.float32)  7.53 us
    all_to_all x1, starting transfers between devices, per_device(): lax.all_to_all(slc, 'date', split_axis=2, concat_axis=0, tiled=True)  7.41 us
    gather x1, local copies, waits for them, and re-layouts, per_device(): second = jnp.take(stripes, pairs[:, 1], axis=0)  3.56 us
    unnamed x5, local copies, waits for them, and re-layouts  2.41 us
    gather x1, local copies, waits for them, and re-layouts, per_device(): first = jnp.take(stripes, pairs[:, 0], axis=0)  2.36 us
    sub x1, other arithmetic, coherence(): cross = first[:, 1] * second[:, 0] - first[:, 0] * second[:, 1]  1.62 us
    dot_general x1, matrix products, coherence(): looked = jnp.dot(rowsum, window, precision=lax.Precision.HIGHEST)  1.03 us
  transfers between devices with their start and end apart: 1, of which 1 were waited for; matrix products, arithmetic and copies ran while one was open for 0% of the time, Pallas kernels for 0%

commit v1 on v0

--- a/solution.py
+++ b/solution.py
@@ -5,6 +5,29 @@
 
 LOOK_R = 4
 LOOK_C = 16
+
+
+def cut_along(x, dim, size):
+    lengths = x.shape
+    pieces = x.reshape(*lengths[:dim], size, lengths[dim] // size, *lengths[dim + 1 :])
+    return jnp.moveaxis(pieces, dim, 0)
+
+
+def laid_out(parts, dim):
+    parts = jnp.moveaxis(parts, 0, dim)
+    lengths = parts.shape
+    return parts.reshape(*lengths[:dim], lengths[dim] * lengths[dim + 1], *lengths[dim + 2 :])
+
+
+def swapped_with_each(x, axis, split_dim, concat_dim):
+    size, index = (lax.axis_size(axis), lax.axis_index(axis))
+    blocks = cut_along(x, split_dim, size)
+    outs = [blocks[index]]
+    for step in range(1, size):
+        sent = blocks[index ^ step]
+        outs.append(lax.ppermute(sent, axis, [(i, i ^ step) for i in range(size)]))
+    blocks = jnp.stack(outs)[index ^ jnp.arange(size)]
+    return laid_out(blocks, concat_dim)
 
 
 def coherence(first, second):
@@ -30,7 +53,7 @@
 
 
 def per_device(slc, pairs, inverse):
-    stripes = lax.all_to_all(slc, "date", split_axis=2, concat_axis=0, tiled=True)
+    stripes = swapped_with_each(slc, "date", 2, 0)
     first = jnp.take(stripes, pairs[:, 0], axis=0)
     second = jnp.take(stripes, pairs[:, 1], axis=0)
     proxy = coherence(first, second)

time: 42.2 us -> 48.5 us (1.15)
  starting transfers between devices: 7.41 us -> 22.7 us
  waiting for transfers between devices: 14.2 us -> 5.89 us
  other arithmetic: 9.83 us -> 8.77 us
    ppermute x0 -> x15, starting transfers between devices: none -> 22.7 us  [swapped_with_each(): outs.append(lax.ppermute(sent, axis, [(i, i ^ step) for i in range(size)]))]
    all_to_all x1 -> x0, waiting for transfers between devices: 14.2 us -> none  [per_device(): lax.all_to_all(slc, 'date', split_axis=2, concat_axis=0, tiled=True)]
    all_to_all x1 -> x0, starting transfers between devices: 7.41 us -> none  [per_device(): lax.all_to_all(slc, 'date', split_axis=2, concat_axis=0, tiled=True)]
    ppermute x0 -> x15, waiting for transfers between devices: none -> 5.89 us  [swapped_with_each(): outs.append(lax.ppermute(sent, axis, [(i, i ^ step) for i in range(size)]))]
    convert_element_type x1, other arithmetic: 7.53 us -> 2.44 us  [coherence(): second = second.astype(jnp.float32)]
    convert_element_type x0 -> x1, other arithmetic: none -> 4.03 us  [coherence(): first = first.astype(jnp.float32)]
    unnamed x5 -> x19, local copies, waits for them, and re-layouts: 2.41 us -> 0.33 us
    reshape x0 -> x1, local copies, waits for them, and re-layouts: none -> 1.26 us  [cut_along(): x.reshape(*lengths[:dim], size, lengths[dim] // size, *lengths[dim + 1:])]
  transfers between devices with their start and end apart: 1 -> 15, of which waited for: 1 -> 3; matrix products, arithmetic and copies ran while one was open for 0% -> 1% of each run, Pallas kernels for 0% -> 0%
where the time goes in v1:
time: 48.5 us; the launch traced here: 48.3 us
  starting transfers between devices  22.7 us (47%)
  local copies, waits for them, and re-layouts  9.45 us (19%)
  other arithmetic  8.77 us (18%)
  waiting for transfers between devices  5.89 us (12%)
  matrix products  1.16 us (2%)
    ppermute x15, starting transfers between devices, swapped_with_each(): outs.append(lax.ppermute(sent, axis, [(i, i ^ step) for i in range(size)]))  22.7 us
    ppermute x15, waiting for transfers between devices, swapped_with_each(): outs.append(lax.ppermute(sent, axis, [(i, i ^ step) for i in range(size)]))  5.89 us
    convert_element_type x1, other arithmetic, coherence(): first = first.astype(jnp.float32)  4.03 us
    gather x1, local copies, waits for them, and re-layouts, per_device(): first = jnp.take(stripes, pairs[:, 0], axis=0)  3.57 us
    convert_element_type x1, other arithmetic, coherence(): second = second.astype(jnp.float32)  2.44 us
    gather x1, local copies, waits for them, and re-layouts, per_device(): second = jnp.take(stripes, pairs[:, 1], axis=0)  2.36 us
    sub x1, other arithmetic, coherence(): cross = first[:, 1] * second[:, 0] - first[:, 0] * second[:, 1]  1.62 us
    reshape x1, local copies, waits for them, and re-layouts, cut_along(): x.reshape(*lengths[:dim], size, lengths[dim] // size, *lengths[dim + 1:])  1.26 us
  transfers between devices with their start and end apart: 15, of which 3 were waited for; matrix products, arithmetic and copies ran while one was open for 1% of the time, Pallas kernels for 0%

profile of v1, /device:TPU:0, one launch (start us, length us, event | category | flops | bytes accessed | tf_op | source)
XLA Modules:
  0.0 48.3 jit_solution(15089032739558214178)
XLA Ops:
  0.0 1.3 %reshape.218 = bf16[1,2,16,4,2048]{4,3,2,1,0:T(4,128)(2,1)S(1)} reshape(bf16[1,2,64,2048]{3,2,1,0:T(8,128)(2,1)} %param.5) | data formatting | bytes 1048576 | tf_op jit(solution)/shard_map/reshape | solution.py:12
  1.4 0.3 dynamic-slice_bitcast_fusion
  1.6 0.6 %collective-permute-start = (bf16[1,2,4,2048]{3,2,1,0:T(4,128)(2,1)S(1)}, bf16[1,2,4,2048]{3,2,1,0:T(4,128)(2,1)S(1)}, u32[]{:S(2)}, u32[]{:S(2)}) collective-permute-start(bf16[1,2,4,2048]{3,2,1,0:T(4,128)(2,1)S(1)} %get-tuple-element.27), channel_id=1, source_target_pairs={{0,1},{1,0},{2,3},{3,2},{4,5},{5,4},{6,7},{7,6},{8,9},{9,8},{10,11... | collective-permute-start | bytes 98312 | tf_op jit(solution)/shard_map/ppermute | solution.py:28
  2.2 2.6 %collective-permute-start.1 = (bf16[1,2,4,2048]{3,2,1,0:T(4,128)(2,1)S(1)}, bf16[1,2,4,2048]{3,2,1,0:T(4,128)(2,1)S(1)}, u32[]{:S(2)}, u32[]{:S(2)}) collective-permute-start(bf16[1,2,4,2048]{3,2,1,0:T(4,128)(2,1)S(1)} %get-tuple-element.26), channel_id=1, source_target_pairs={{0,2},{1,3},{2,0},{3,1},{4,6},{5,7},{6,4},{7,5},{8,10},{9,11},{10,... | collective-permute-start | bytes 98312 | tf_op jit(solution)/shard_map/ppermute | solution.py:28
  4.8 1.8 %collective-permute-start.3 = (bf16[1,2,4,2048]{3,2,1,0:T(4,128)(2,1)S(1)}, bf16[1,2,4,2048]{3,2,1,0:T(4,128)(2,1)S(1)}, u32[]{:S(2)}, u32[]{:S(2)}) collective-permute-start(bf16[1,2,4,2048]{3,2,1,0:T(4,128)(2,1)S(1)} %get-tuple-element.24), channel_id=1, source_target_pairs={{0,4},{1,5},{2,6},{3,7},{4,0},{5,1},{6,2},{7,3},{8,12},{9,13},{10,... | collective-permute-start | bytes 98312 | tf_op jit(solution)/shard_map/ppermute | solution.py:28
  6.7 2.7 %collective-permute-start.5 = (bf16[1,2,4,2048]{3,2,1,0:T(4,128)(2,1)S(1)}, bf16[1,2,4,2048]{3,2,1,0:T(4,128)(2,1)S(1)}, u32[]{:S(2)}, u32[]{:S(2)}) collective-permute-start(bf16[1,2,4,2048]{3,2,1,0:T(4,128)(2,1)S(1)} %get-tuple-element.22), channel_id=1, source_target_pairs={{0,6},{1,7},{2,4},{3,5},{4,2},{5,3},{6,0},{7,1},{8,14},{9,15},{10,... | collective-permute-start | bytes 98312 | tf_op jit(solution)/shard_map/ppermute | solution.py:28
  9.6 2.7 %collective-permute-start.7 = (bf16[1,2,4,2048]{3,2,1,0:T(4,128)(2,1)S(1)}, bf16[1,2,4,2048]{3,2,1,0:T(4,128)(2,1)S(1)}, u32[]{:S(2)}, u32[]{:S(2)}) collective-permute-start(bf16[1,2,4,2048]{3,2,1,0:T(4,128)(2,1)S(1)} %get-tuple-element.20), channel_id=1, source_target_pairs={{0,8},{1,9},{2,10},{3,11},{4,12},{5,13},{6,14},{7,15},{8,0},{9,1},... | collective-permute-start | bytes 98312 | tf_op jit(solution)/shard_map/ppermute | solution.py:28
  12.4 0.1 collective-permute-start.8
  12.6 3.6 %collective-permute-start.9 = (bf16[1,2,4,2048]{3,2,1,0:T(4,128)(2,1)S(1)}, bf16[1,2,4,2048]{3,2,1,0:T(4,128)(2,1)S(1)}, u32[]{:S(2)}, u32[]{:S(2)}) collective-permute-start(bf16[1,2,4,2048]{3,2,1,0:T(4,128)(2,1)S(1)} %get-tuple-element.18), channel_id=1, source_target_pairs={{0,10},{1,11},{2,8},{3,9},{4,14},{5,15},{6,12},{7,13},{8,2},{9,3},... | collective-permute-start | bytes 98312 | tf_op jit(solution)/shard_map/ppermute | solution.py:28
  16.3 3.6 %collective-permute-start.11 = (bf16[1,2,4,2048]{3,2,1,0:T(4,128)(2,1)S(1)}, bf16[1,2,4,2048]{3,2,1,0:T(4,128)(2,1)S(1)}, u32[]{:S(2)}, u32[]{:S(2)}) collective-permute-start(bf16[1,2,4,2048]{3,2,1,0:T(4,128)(2,1)S(1)} %get-tuple-element.16), channel_id=1, source_target_pairs={{0,12},{1,13},{2,14},{3,15},{4,8},{5,9},{6,10},{7,11},{8,4},{9,5},... | collective-permute-start | bytes 98312 | tf_op jit(solution)/shard_map/ppermute | solution.py:28
  20.1 4.5 %collective-permute-start.13 = (bf16[1,2,4,2048]{3,2,1,0:T(4,128)(2,1)S(1)}, bf16[1,2,4,2048]{3,2,1,0:T(4,128)(2,1)S(1)}, u32[]{:S(2)}, u32[]{:S(2)}) collective-permute-start(bf16[1,2,4,2048]{3,2,1,0:T(4,128)(2,1)S(1)} %get-tuple-element.14), channel_id=1, source_target_pairs={{0,14},{1,15},{2,12},{3,13},{4,10},{5,11},{6,8},{7,9},{8,6},{9,7},... | collective-permute-start | bytes 98312 | tf_op jit(solution)/shard_map/ppermute | solution.py:28
  24.9 0.5 collective-permute-done.12
  25.4 2.0 %collective-permute-done.13 = bf16[1,2,4,2048]{3,2,1,0:T(4,128)(2,1)S(1)} collective-permute-done((bf16[1,2,4,2048]{3,2,1,0:T(4,128)(2,1)S(1)}, bf16[1,2,4,2048]{3,2,1,0:T(4,128)(2,1)S(1)}, u32[]{:S(2)}, u32[]{:S(2)}) %collective-permute-start.13) | collective-permute-done | bytes 32800 | tf_op jit(solution)/shard_map/ppermute | solution.py:28
  27.3 3.4 %collective-permute-done.14 = bf16[1,2,4,2048]{3,2,1,0:T(4,128)(2,1)S(1)} collective-permute-done((bf16[1,2,4,2048]{3,2,1,0:T(4,128)(2,1)S(1)}, bf16[1,2,4,2048]{3,2,1,0:T(4,128)(2,1)S(1)}, u32[]{:S(2)}, u32[]{:S(2)}) %collective-permute-start.14) | collective-permute-done | bytes 32800 | tf_op jit(solution)/shard_map/ppermute | solution.py:28
  30.8 1.0 %gather_fusion = bf16[16,2,4,2048]{3,2,1,0:T(4,128)(2,1)S(1)} fusion(bf16[16,2,4,2048]{3,2,1,0:T(4,128)(2,1)S(1)} %bitcast.91, s32[1024]{0:T(1024)S(1)} %pad_clamp_fusion.2), kind=kCustom, calls=%fused_computation.2 | custom fusion | bytes 1048640 | tf_op jit(solution)/shard_map/gather | solution.py:29
  31.8 3.6 %gather_fusion.1 = bf16[64,2,4,2048]{3,2,1,0:T(4,128)(2,1)} fusion(bf16[16,2,4,2048]{3,2,1,0:T(4,128)(2,1)S(1)} %gather_fusion, s32[1024]{0:T(1024)S(1)} %get-tuple-element.31), kind=kCustom, calls=%fused_computation.clone | custom fusion | bytes 4194560 | tf_op jit(solution)/shard_map/jit(_take)/gather | solution.py:57
  35.4 2.4 %gather_fusion.2 = bf16[64,2,4,2048]{3,2,1,0:T(4,128)(2,1)S(1)} fusion(bf16[16,2,4,2048]{3,2,1,0:T(4,128)(2,1)S(1)} %gather_fusion, s32[1024]{0:T(1024)S(1)} %get-tuple-element.30), kind=kCustom, calls=%fused_computation.1.clone | custom fusion | bytes 4194560 | tf_op jit(solution)/shard_map/jit(_take)/gather | solution.py:58
  37.7 4.0 %fusion.1 = f32[64,2,4,2048]{3,0,2,1:T(8,128)S(1)} fusion(bf16[64,2,4,2048]{3,2,1,0:T(4,128)(2,1)} %gather_fusion.1, pred[64]{0:T(512)(128)(4,1)S(1)} %get-tuple-element.6), kind=kLoop, calls=%fused_computation.7 | loop fusion | flops 2097152 | bytes 6291520 | tf_op jit(solution)/shard_map/convert_element_type | solution.py:34
  41.8 2.4 %fusion = f32[64,2,4,2048]{3,0,2,1:T(8,128)S(1)} fusion(bf16[64,2,4,2048]{3,2,1,0:T(4,128)(2,1)S(1)} %gather_fusion.2, pred[64]{0:T(512)(128)(4,1)S(1)} %get-tuple-element.28), kind=kLoop, calls=%fused_computation.5 | loop fusion | flops 2097152 | bytes 6291520 | tf_op jit(solution)/shard_map/convert_element_type | solution.py:35
  44.2 1.6 %subtract_bitcast_fusion = (f32[1,64,4,2048]{3,1,2,0:T(8,128)S(1)}, f32[1,64,4,2048]{3,1,2,0:T(8,128)S(1)}, f32[1,64,4,2048]{3,1,2,0:T(8,128)S(1)}) fusion(f32[64,2,4,2048]{3,0,2,1:T(8,128)S(1)} %fusion, f32[64,2,4,2048]{3,0,2,1:T(8,128)S(1)} %fusion.1), kind=kLoop, calls=%fused_computation.10 | loop fusion | flops 4718592 | bytes 14680064 | tf_op jit(solution)/shard_map/sub | solution.py:36
  45.8 0.7 %maximum_reduce_fusion = f32[3,64,2048]{2,1,0:T(8,128)S(1)} fusion(f32[1,64,4,2048]{3,1,2,0:T(8,128)S(1)} %get-tuple-element.12, f32[1,64,4,2048]{3,1,2,0:T(8,128)S(1)} %get-tuple-element.11, f32[1,64,4,2048]{3,1,2,0:T(8,128)S(1)} %get-tuple-element.10), kind=kLoop, calls=%fused_computation.3 | loop fusion | flops 4325376 | bytes 7864320 | tf_op jit(solution)/shard_map/reduce_sum | solution.py:41
  46.5 1.0 %fusion.3 = f32[3,64,128]{2,1,0:T(8,128)S(1)} fusion(f32[3,64,2048]{2,1,0:T(8,128)S(1)} %maximum_reduce_fusion, s32[2048]{0:T(1024)S(1)} %add_select_fusion), kind=kOutput, calls=%fused_computation.14 | convolution fusion | flops 604241920 | bytes 1679360 | tf_op jit(solution)/shard_map/dot_general | solution.py:45
  47.5 0.1 convolution_bitcast_fusion
  47.7 0.6 %copy.15 = f32[15,1,128]{2,1,0:T(1,128)} copy(f32[15,1,128]{2,0,1:T(8,128)S(1)} %convolution_bitcast_fusion) | data formatting | bytes 15360 | tf_op jit(solution)/shard_map/sp,pxy->sxy/dot_general | solution.py:50
  (43 shorter events, 0.9 us)
Async XLA Ops:
  0.0 47.5 %copy-start = (bf16[15,64]{1,0:T(8,128)(2,1)S(1)}, bf16[15,64]{1,0:T(8,128)(2,1)}, u32[]{:S(2)}) copy-start(bf16[15,64]{1,0:T(8,128)(2,1)} %param.7) | copy-start | bytes 5764
  0.0 6.7 %copy-start.1 = (s32[64,2]{0,1:T(2,128)S(1)}, s32[64,2]{0,1:T(2,128)}, u32[]{:S(2)}) copy-start(s32[64,2]{0,1:T(2,128)} %param.6) | copy-start | bytes 1540
  1.6 5.1 %collective-permute-start = (bf16[1,2,4,2048]{3,2,1,0:T(4,128)(2,1)S(1)}, bf16[1,2,4,2048]{3,2,1,0:T(4,128)(2,1)S(1)}, u32[]{:S(2)}, u32[]{:S(2)}) collective-permute-start(bf16[1,2,4,2048]{3,2,1,0:T(4,128)(2,1)S(1)} %get-tuple-element.27), channel_id=1, source_target_pairs={{0,1},{1,0},{2,3},{3,2},{4,5},{5,4},{6,7},{7,6},{8,9},{9,8},{10,11... | collective-permute-start | bytes 98312 | tf_op jit(solution)/shard_map/ppermute | solution.py:28
  2.2 7.3 %collective-permute-start.1 = (bf16[1,2,4,2048]{3,2,1,0:T(4,128)(2,1)S(1)}, bf16[1,2,4,2048]{3,2,1,0:T(4,128)(2,1)S(1)}, u32[]{:S(2)}, u32[]{:S(2)}) collective-permute-start(bf16[1,2,4,2048]{3,2,1,0:T(4,128)(2,1)S(1)} %get-tuple-element.26), channel_id=1, source_target_pairs={{0,2},{1,3},{2,0},{3,1},{4,6},{5,7},{6,4},{7,5},{8,10},{9,11},{10,... | collective-permute-start | bytes 98312 | tf_op jit(solution)/shard_map/ppermute | solution.py:28
  4.8 4.8 %collective-permute-start.2 = (bf16[1,2,4,2048]{3,2,1,0:T(4,128)(2,1)S(1)}, bf16[1,2,4,2048]{3,2,1,0:T(4,128)(2,1)S(1)}, u32[]{:S(2)}, u32[]{:S(2)}) collective-permute-start(bf16[1,2,4,2048]{3,2,1,0:T(4,128)(2,1)S(1)} %get-tuple-element.25), channel_id=1, source_target_pairs={{0,3},{1,2},{2,1},{3,0},{4,7},{5,6},{6,5},{7,4},{8,11},{9,10},{10,... | collective-permute-start | bytes 98312 | tf_op jit(solution)/shard_map/ppermute | solution.py:28
  4.8 7.6 %collective-permute-start.3 = (bf16[1,2,4,2048]{3,2,1,0:T(4,128)(2,1)S(1)}, bf16[1,2,4,2048]{3,2,1,0:T(4,128)(2,1)S(1)}, u32[]{:S(2)}, u32[]{:S(2)}) collective-permute-start(bf16[1,2,4,2048]{3,2,1,0:T(4,128)(2,1)S(1)} %get-tuple-element.24), channel_id=1, source_target_pairs={{0,4},{1,5},{2,6},{3,7},{4,0},{5,1},{6,2},{7,3},{8,12},{9,13},{10,... | collective-permute-start | bytes 98312 | tf_op jit(solution)/shard_map/ppermute | solution.py:28
  6.6 6.0 %collective-permute-start.4 = (bf16[1,2,4,2048]{3,2,1,0:T(4,128)(2,1)S(1)}, bf16[1,2,4,2048]{3,2,1,0:T(4,128)(2,1)S(1)}, u32[]{:S(2)}, u32[]{:S(2)}) collective-permute-start(bf16[1,2,4,2048]{3,2,1,0:T(4,128)(2,1)S(1)} %get-tuple-element.23), channel_id=1, source_target_pairs={{0,5},{1,4},{2,7},{3,6},{4,1},{5,0},{6,3},{7,2},{8,13},{9,12},{10,... | collective-permute-start | bytes 98312 | tf_op jit(solution)/shard_map/ppermute | solution.py:28
  6.7 9.4 %collective-permute-start.5 = (bf16[1,2,4,2048]{3,2,1,0:T(4,128)(2,1)S(1)}, bf16[1,2,4,2048]{3,2,1,0:T(4,128)(2,1)S(1)}, u32[]{:S(2)}, u32[]{:S(2)}) collective-permute-start(bf16[1,2,4,2048]{3,2,1,0:T(4,128)(2,1)S(1)} %get-tuple-element.22), channel_id=1, source_target_pairs={{0,6},{1,7},{2,4},{3,5},{4,2},{5,3},{6,0},{7,1},{8,14},{9,15},{10,... | collective-permute-start | bytes 98312 | tf_op jit(solution)/shard_map/ppermute | solution.py:28
  9.5 6.8 %collective-permute-start.6 = (bf16[1,2,4,2048]{3,2,1,0:T(4,128)(2,1)S(1)}, bf16[1,2,4,2048]{3,2,1,0:T(4,128)(2,1)S(1)}, u32[]{:S(2)}, u32[]{:S(2)}) collective-permute-start(bf16[1,2,4,2048]{3,2,1,0:T(4,128)(2,1)S(1)} %get-tuple-element.21), channel_id=1, source_target_pairs={{0,7},{1,6},{2,5},{3,4},{4,3},{5,2},{6,1},{7,0},{8,15},{9,14},{10,... | collective-permute-start | bytes 98312 | tf_op jit(solution)/shard_map/ppermute | solution.py:28
  9.6 10.4 %collective-permute-start.7 = (bf16[1,2,4,2048]{3,2,1,0:T(4,128)(2,1)S(1)}, bf16[1,2,4,2048]{3,2,1,0:T(4,128)(2,1)S(1)}, u32[]{:S(2)}, u32[]{:S(2)}) collective-permute-start(bf16[1,2,4,2048]{3,2,1,0:T(4,128)(2,1)S(1)} %get-tuple-element.20), channel_id=1, source_target_pairs={{0,8},{1,9},{2,10},{3,11},{4,12},{5,13},{6,14},{7,15},{8,0},{9,1},... | collective-permute-start | bytes 98312 | tf_op jit(solution)/shard_map/ppermute | solution.py:28
  12.4 7.7 %collective-permute-start.8 = (bf16[1,2,4,2048]{3,2,1,0:T(4,128)(2,1)S(1)}, bf16[1,2,4,2048]{3,2,1,0:T(4,128)(2,1)S(1)}, u32[]{:S(2)}, u32[]{:S(2)}) collective-permute-start(bf16[1,2,4,2048]{3,2,1,0:T(4,128)(2,1)S(1)} %get-tuple-element.19), channel_id=1, source_target_pairs={{0,9},{1,8},{2,11},{3,10},{4,13},{5,12},{6,15},{7,14},{8,1},{9,0},... | collective-permute-start | bytes 98312 | tf_op jit(solution)/shard_map/ppermute | solution.py:28
  12.6 12.1 %collective-permute-start.9 = (bf16[1,2,4,2048]{3,2,1,0:T(4,128)(2,1)S(1)}, bf16[1,2,4,2048]{3,2,1,0:T(4,128)(2,1)S(1)}, u32[]{:S(2)}, u32[]{:S(2)}) collective-permute-start(bf16[1,2,4,2048]{3,2,1,0:T(4,128)(2,1)S(1)} %get-tuple-element.18), channel_id=1, source_target_pairs={{0,10},{1,11},{2,8},{3,9},{4,14},{5,15},{6,12},{7,13},{8,2},{9,3},... | collective-permute-start | bytes 98312 | tf_op jit(solution)/shard_map/ppermute | solution.py:28
  16.2 8.6 %collective-permute-start.10 = (bf16[1,2,4,2048]{3,2,1,0:T(4,128)(2,1)S(1)}, bf16[1,2,4,2048]{3,2,1,0:T(4,128)(2,1)S(1)}, u32[]{:S(2)}, u32[]{:S(2)}) collective-permute-start(bf16[1,2,4,2048]{3,2,1,0:T(4,128)(2,1)S(1)} %get-tuple-element.17), channel_id=1, source_target_pairs={{0,11},{1,10},{2,9},{3,8},{4,15},{5,14},{6,13},{7,12},{8,3},{9,2},... | collective-permute-start | bytes 98312 | tf_op jit(solution)/shard_map/ppermute | solution.py:28
  16.3 8.5 %collective-permute-start.11 = (bf16[1,2,4,2048]{3,2,1,0:T(4,128)(2,1)S(1)}, bf16[1,2,4,2048]{3,2,1,0:T(4,128)(2,1)S(1)}, u32[]{:S(2)}, u32[]{:S(2)}) collective-permute-start(bf16[1,2,4,2048]{3,2,1,0:T(4,128)(2,1)S(1)} %get-tuple-element.16), channel_id=1, source_target_pairs={{0,12},{1,13},{2,14},{3,15},{4,8},{5,9},{6,10},{7,11},{8,4},{9,5},... | collective-permute-start | bytes 98312 | tf_op jit(solution)/shard_map/ppermute | solution.py:28
  20.0 5.3 %collective-permute-start.12 = (bf16[1,2,4,2048]{3,2,1,0:T(4,128)(2,1)S(1)}, bf16[1,2,4,2048]{3,2,1,0:T(4,128)(2,1)S(1)}, u32[]{:S(2)}, u32[]{:S(2)}) collective-permute-start(bf16[1,2,4,2048]{3,2,1,0:T(4,128)(2,1)S(1)} %get-tuple-element.15), channel_id=1, source_target_pairs={{0,13},{1,12},{2,15},{3,14},{4,9},{5,8},{6,11},{7,10},{8,5},{9,4},... | collective-permute-start | bytes 98312 | tf_op jit(solution)/shard_map/ppermute | solution.py:28
  20.1 7.2 %collective-permute-start.13 = (bf16[1,2,4,2048]{3,2,1,0:T(4,128)(2,1)S(1)}, bf16[1,2,4,2048]{3,2,1,0:T(4,128)(2,1)S(1)}, u32[]{:S(2)}, u32[]{:S(2)}) collective-permute-start(bf16[1,2,4,2048]{3,2,1,0:T(4,128)(2,1)S(1)} %get-tuple-element.14), channel_id=1, source_target_pairs={{0,14},{1,15},{2,12},{3,13},{4,10},{5,11},{6,8},{7,9},{8,6},{9,7},... | collective-permute-start | bytes 98312 | tf_op jit(solution)/shard_map/ppermute | solution.py:28
  24.7 6.1 %collective-permute-start.14 = (bf16[1,2,4,2048]{3,2,1,0:T(4,128)(2,1)S(1)}, bf16[1,2,4,2048]{3,2,1,0:T(4,128)(2,1)S(1)}, u32[]{:S(2)}, u32[]{:S(2)}) collective-permute-start(bf16[1,2,4,2048]{3,2,1,0:T(4,128)(2,1)S(1)} %get-tuple-element.13), channel_id=1, source_target_pairs={{0,15},{1,14},{2,13},{3,12},{4,11},{5,10},{6,9},{7,8},{8,7},{9,6},... | collective-permute-start | bytes 98312 | tf_op jit(solution)/shard_map/ppermute | solution.py:28
